TPU v7x, 256 devices: a whole 4x4x8 slice. The times are simulated.
256 devices in a mesh: req: 64 (over z, y, core), tp: 4 (over x).
Axes of the slice: x: 4, y: 4, z: 8, core: 2. Of those that a mesh axis runs over, the one named last changes fastest.
Arguments:
- hidden_in: bfloat16 [8192, 2048], P('req'), may hold values from -6 to 6
- attn_gain: float32 [2048], replicated, may hold values from 0.1 to 1.9
- w_query: bfloat16 [2048, 3072], P(None, 'tp'), may hold values from -0.125 to 0.125
- w_latent: bfloat16 [2048, 576], P(None, 'tp'), may hold values from -0.125 to 0.125
- kv_gain: float32 [512], replicated, may hold values from 0.1 to 1.9
- w_key_up: bfloat16 [512, 2048], P(None, 'tp'), may hold values from -0.25 to 0.25
- w_value_up: bfloat16 [512, 2048], P(None, 'tp'), may hold values from -0.25 to 0.25
- w_out: bfloat16 [2048, 2048], P('tp'), may hold values from -0.125 to 0.125
- moe_gain: float32 [2048], replicated, may hold values from 0.1 to 1.9
- w_gate: bfloat16 [64, 2048, 1408], P('req', None, 'tp'), may hold values from -0.125 to 0.125
- w_up: bfloat16 [64, 2048, 1408], P('req', None, 'tp'), may hold values from -0.125 to 0.125
- w_down: bfloat16 [64, 1408, 2048], P('req', 'tp'), may hold values from -0.15625 to 0.15625
- latent_cache: bfloat16 [2048, 64, 576], P('req'), may hold values from -3000 to 3000
- page_table: int32 [256, 8], P('req'), may hold values from 0 to 7, as said below
- cache_len: int32 [256], P('req'), may hold values from 1 to 512, 65536 in all
- parents: int32 [256, 3, 8], P('req'), may hold values from 0 to 7
- routes: int32 [8192, 6], P('req'), may hold values from 0 to 63, all different within a row; in each aligned block of 128 rows (0 to 127, 128 to 255, ...) at most 24 rows name the same one
- route_weights: float32 [8192, 6], P('req'), may hold values from 0.1 to 1
Outputs:
- layer_out: bfloat16 [8192, 2048], P('req', 'tp')
Inputs may be any that keep to these rules, and one draw needn't show every extreme that they name: `page_table`: each request's row lists the 8 pages of that request's block of the pool, each once. `routes`: each row names 6 different experts; in the rows of one index of req no expert is named more than 24 times, a bound that some block reaches.
All inputs are finite; a program needn't handle non-finite values. No bound on the sum of `cache_len` on one device may be relied on, other than what follows from the above.
Results may differ from a plain program's by a relative error of at most 0.015.
The roundings to bfloat16 on the way count: a program that leaves them out, or rounds other values in their place, can miss the bound.
Values may be sent and summed in bfloat16 or wider, within the bound.
No kernel may reach another device: no remote copies, remote signals or barrier semaphores. Data moves between devices by JAX's collectives and lax.ppermute only.
A program may use at most 128 MiB of HBM per device.

v0:
```python
import jax
import jax.numpy as jnp
from jax import lax
from jax.sharding import PartitionSpec as P

D = 2048
NOPE = 128
ROPE = 64
VDIM = 128
LATENT = 512
TOPK = 6
EXP_DEV = 1
BEAMS = 8
STEPS = 4
PAGE = 64
PAGES = 8
eps = 1e-06
rope_base = 50000.0


def rms_scale(values):
    return lax.rsqrt(jnp.mean(values * values, axis=-1, keepdims=True) + eps)


def rotate(values, cos_val, sin_val):
    half_rope = values.shape[-1] // 2
    first = values[..., :half_rope]
    second = values[..., half_rope:]
    return jnp.concatenate(
        [first * cos_val - second * sin_val, second * cos_val + first * sin_val], axis=-1
    )


def expert_math(arrived, gate_w, up_w, down_w):
    gate_val = jnp.einsum("nesd,edf->nesf", arrived, gate_w, preferred_element_type=jnp.float32)
    up_val = jnp.einsum("nesd,edf->nesf", arrived, up_w, preferred_element_type=jnp.float32)
    active = (jax.nn.silu(gate_val) * up_val).astype(jnp.bfloat16)
    return jnp.einsum("nesf,efd->nesd", active, down_w, preferred_element_type=jnp.float32)


def send_home(shares):
    return lax.all_to_all(shares, "req", split_axis=0, concat_axis=0, tiled=True)


def local(
    hidden_in,
    attn_gain,
    w_query,
    w_latent,
    kv_gain,
    w_key_up,
    w_value_up,
    w_out,
    moe_gain,
    w_gate,
    w_up,
    w_down,
    latent_cache,
    page_table,
    cache_len,
    parents,
    routes,
    route_weights,
):
    highest = lax.Precision.HIGHEST
    row_count = hidden_in.shape[0]
    req_local = cache_len.shape[0]
    heads_local = w_value_up.shape[1] // VDIM
    tp_count = lax.axis_size("tp")
    req_count = lax.axis_size("req")
    col_share = D // tp_count
    max_len = PAGES * PAGE
    hidden_f = hidden_in.astype(jnp.float32)
    normed = (hidden_f * rms_scale(hidden_f) * attn_gain).astype(jnp.bfloat16)
    positions = (
        cache_len.astype(jnp.float32)[:, None, None]
        + jnp.arange(STEPS, dtype=jnp.float32)[None, :, None]
        + jnp.zeros((1, 1, BEAMS), jnp.float32)
    ).reshape(row_count)
    frequency = rope_base ** (-2.0 * jnp.arange(ROPE // 2, dtype=jnp.float32) / ROPE)
    angles = positions[:, None] * frequency[None, :]
    cos_val = jnp.cos(angles)
    sin_val = jnp.sin(angles)
    queries = jnp.dot(normed, w_query, preferred_element_type=jnp.float32).reshape(
        row_count, heads_local, NOPE + ROPE
    )
    q_nope = queries[:, :, :NOPE].astype(jnp.bfloat16)
    q_rope = rotate(queries[:, :, NOPE:], cos_val[:, None, :], sin_val[:, None, :]).astype(
        jnp.bfloat16
    )
    kv_part = jnp.dot(normed, w_latent, preferred_element_type=jnp.float32)
    kv_all = lax.all_gather(kv_part, "tp", axis=1, tiled=True)
    new_lat = kv_all[:, :LATENT] * rms_scale(kv_all[:, :LATENT]) * kv_gain
    new_rope = rotate(kv_all[:, LATENT:], cos_val, sin_val)
    new_keys = jnp.concatenate([new_lat, new_rope], axis=1).astype(jnp.bfloat16)
    key_up = w_key_up.reshape(LATENT, heads_local, NOPE)
    q_lat = jnp.einsum("nhc,lhc->nhl", q_nope, key_up, preferred_element_type=jnp.float32).astype(
        jnp.bfloat16
    )
    query_key = jnp.concatenate([q_lat, q_rope], axis=2)
    pool_index = (jnp.arange(req_local, dtype=jnp.int32) * PAGES)[:, None] + page_table
    cache_keys = jnp.take(latent_cache, pool_index.reshape(-1), axis=0).reshape(
        req_local, max_len, LATENT + ROPE
    )
    live_mask = jnp.arange(max_len, dtype=jnp.int32)[None, :] < cache_len[:, None]
    score_scale = (NOPE + ROPE) ** (-0.5)
    grouped = query_key.reshape(req_local, STEPS * BEAMS * heads_local, LATENT + ROPE)
    s_cache = (
        jnp.einsum("rqd,rld->rql", grouped, cache_keys, preferred_element_type=jnp.float32)
        * score_scale
    )
    s_cache = jnp.where(live_mask[:, None, :], s_cache, -jnp.inf).reshape(
        req_local, STEPS, BEAMS, heads_local, max_len
    )
    fresh = new_keys.reshape(req_local, STEPS, BEAMS, LATENT + ROPE).astype(jnp.float32)
    parent_hot = (parents[..., None] == jnp.arange(BEAMS, dtype=jnp.int32)).astype(jnp.float32)
    identity = jnp.broadcast_to(jnp.eye(BEAMS, dtype=jnp.float32), (req_local, BEAMS, BEAMS))
    tail_rows = []
    for step_index in range(STEPS):
        lineage = identity
        pieces = [None] * STEPS
        for earlier in range(step_index, -1, -1):
            pieces[earlier] = jnp.einsum(
                "rba,rad->rbd", lineage, fresh[:, earlier], precision=highest
            )
            if earlier > 0:
                lineage = jnp.einsum(
                    "rba,rac->rbc", lineage, parent_hot[:, earlier - 1], precision=highest
                )
        for later in range(step_index + 1, STEPS):
            pieces[later] = jnp.zeros_like(pieces[0])
        tail_rows.append(jnp.stack(pieces, axis=2))
    tail_keys = jnp.stack(tail_rows, axis=1).astype(jnp.bfloat16)
    queries_tail = query_key.reshape(req_local, STEPS, BEAMS, heads_local, LATENT + ROPE)
    s_tail = (
        jnp.einsum(
            "rsbhd,rsbjd->rsbhj", queries_tail, tail_keys, preferred_element_type=jnp.float32
        )
        * score_scale
    )
    causal = jnp.arange(STEPS)[None, :] <= jnp.arange(STEPS)[:, None]
    s_tail = jnp.where(causal[None, :, None, None, :], s_tail, -jnp.inf)
    top_score = jnp.maximum(jnp.max(s_cache, axis=-1), jnp.max(s_tail, axis=-1))
    e_cache = jnp.exp(s_cache - top_score[..., None])
    e_tail = jnp.exp(s_tail - top_score[..., None])
    total = jnp.sum(e_cache, axis=-1) + jnp.sum(e_tail, axis=-1)
    p_cache = (e_cache / total[..., None]).astype(jnp.bfloat16)
    p_tail = (e_tail / total[..., None]).astype(jnp.bfloat16)
    context = jnp.einsum(
        "rsbhl,rld->rsbhd", p_cache, cache_keys[..., :LATENT], preferred_element_type=jnp.float32
    )
    context = context + jnp.einsum(
        "rsbhj,rsbjd->rsbhd", p_tail, tail_keys[..., :LATENT], preferred_element_type=jnp.float32
    )
    context = context.astype(jnp.bfloat16).reshape(row_count, heads_local, LATENT)
    value_up = w_value_up.reshape(LATENT, heads_local, VDIM)
    head_out = (
        jnp.einsum("nhl,lhv->nhv", context, value_up, preferred_element_type=jnp.float32)
        .astype(jnp.bfloat16)
        .reshape(row_count, heads_local * VDIM)
    )
    attn_part = jnp.dot(head_out, w_out, preferred_element_type=jnp.float32)
    expert_count = EXP_DEV * req_count
    capacity = min(row_count, 2 * row_count * TOPK // expert_count)
    slot_count = expert_count * capacity
    picks = routes.reshape(-1)
    pick_hot = (picks[:, None] == jnp.arange(expert_count, dtype=jnp.int32)[None, :]).astype(
        jnp.int32
    )
    before = jnp.cumsum(pick_hot, axis=0) - pick_hot
    ranks = jnp.sum(before * pick_hot, axis=1)
    slot_of = picks * capacity + ranks
    slot_hot = (slot_of[:, None] == jnp.arange(slot_count, dtype=jnp.int32)[None, :]).reshape(
        row_count, TOPK, slot_count
    )
    gather_rows = jnp.sum(slot_hot.astype(jnp.int32), axis=1).astype(jnp.bfloat16)
    weight_rows = jnp.sum(jnp.where(slot_hot, route_weights[:, :, None], 0.0), axis=1)
    tp_index = lax.axis_index("tp")
    col_start = tp_index * col_share
    attn_full = lax.psum(attn_part, "tp")
    resid_full = hidden_f + attn_full
    moe_in = (resid_full * rms_scale(resid_full) * moe_gain).astype(jnp.bfloat16)
    placed = jnp.dot(gather_rows.T, moe_in, preferred_element_type=jnp.float32).astype(jnp.bfloat16)
    partial_out = expert_math(
        lax.all_to_all(
            placed.reshape(req_count, EXP_DEV, capacity, moe_in.shape[1]),
            "req",
            split_axis=0,
            concat_axis=0,
            tiled=True,
        ),
        w_gate,
        w_up,
        w_down,
    )
    shares = lax.psum_scatter(partial_out, "tp", scatter_dimension=3, tiled=True)
    returned = send_home(shares.astype(jnp.bfloat16))
    resid_cols = lax.dynamic_slice_in_dim(resid_full, col_start, col_share, 1)
    combined = jnp.dot(
        weight_rows, returned.reshape(slot_count, col_share).astype(jnp.float32), precision=highest
    )
    return (resid_cols + combined).astype(jnp.bfloat16)


def solution(mesh):
    in_specs = (
        P("req", None),
        P(),
        P(None, "tp"),
        P(None, "tp"),
        P(),
        P(None, "tp"),
        P(None, "tp"),
        P("tp", None),
        P(),
        P("req", None, "tp"),
        P("req", None, "tp"),
        P("req", "tp", None),
        P("req", None, None),
        P("req", None),
        P("req"),
        P("req", None, None),
        P("req", None),
        P("req", None),
    )
    out_specs = P("req", "tp")
    return jax.shard_map(local, mesh=mesh, in_specs=in_specs, out_specs=out_specs, check_vma=False)
```

profile of v0, /device:TPU:1, one launch (start us, length us, event | category | flops | bytes accessed | tf_op | source)
XLA Modules:
  0.0 477.5 jit_solution(17207747423116017685)
XLA Ops:
  8.2 1.2 fusion.40
  9.5 1.6 fusion.63
  11.1 11.2 %all_gather.3 = f32[128,576]{0,1:T(8,128)S(1)} all-gather(f32[128,144]{0,1:T(8,128)S(1)} %fusion.63), channel_id=1, replica_groups=mesh['req'=64,'tp'=4] {'tp'}, dimensions={1}, use_global_device_ids=true | all-gather | bytes 368640 | tf_op jit(solution)/shard_map/all_gather | solution.py:92
  23.2 1.6 copy.150
  26.4 1.0 pad_maximum_fusion.2
  38.8 2.4 fusion.65
  41.5 1.4 fusion.22
  44.5 1.2 reshape.300
  46.0 4.1 gather_fusion
  50.1 2.1 bitcast_select_fusion
  52.3 2.0 fusion.86
  55.6 3.1 fusion.87
  59.0 1.2 fusion.58
  60.2 2.6 reshape.302
  62.8 1.5 exponential_reduce_fusion
  64.6 1.7 fusion.51
  67.3 1.4 copy.179
  69.1 1.5 fusion.88
  71.2 1.8 reduce-window.6
  74.4 50.8 %all-reduce.2.cloned.1.call-done = f32[128,2048]{1,0:T(8,128)} async-done(((f32[128,2048]{1,0:T(8,128)}), f32[128,2048]{1,0:T(8,128)}) %all-reduce.2.cloned.1.call-update) | async-done | bytes 1048592 | tf_op jit(solution)/shard_map/psum | solution.py:180
  125.1 1.4 multiply_reduce_fusion
  126.6 1.9 convolution_convert_fusion
  128.5 151.6 %all_to_all.10 = bf16[64,1,24,2048]{3,2,1,0:T(8,128)(2,1)S(1)} all-to-all(bf16[64,1,24,2048]{3,2,1,0:T(8,128)(2,1)S(1)} %bitcast.216), channel_id=1, replica_groups=mesh['req'=64,'tp'=4] {'req'}, dimensions={0} | all-to-all | bytes 12582912 | tf_op jit(solution)/shard_map/all_to_all | solution.py:185
  280.1 2.6 copy-done.2
  282.6 5.0 %fusion.2 = f32[64,24,352]{2,1,0:T(8,128)} fusion(bf16[64,1,24,2048]{3,2,1,0:T(8,128)(2,1)S(1)} %all_to_all.10, bf16[1,2048,352]{1,2,0:T(8,128)(2,1)S(1)} %copy-done.25), kind=kOutput, calls=%fused_computation.4 | convolution fusion | flops 2214592512 | bytes 9895936 | tf_op jit(solution)/shard_map/nesd,edf->nesf/dot_general | solution.py:35
  287.7 12.3 %convolution_bitcast_fusion = f32[64,1,24,2048]{3,2,0,1:T(8,128)} fusion(bf16[1,352,2048]{2,1,0:T(8,128)(2,1)S(1)} %copy-done.26, bf16[1,2048,352]{1,2,0:T(8,128)(2,1)} %param.28, bf16[64,1,24,2048]{3,2,1,0:T(8,128)(2,1)} %copy-done.2, f32[64,24,352]{2,1,0:T(8,128)} %fusion.2), kind=kOutput, calls=%fused_computation.6 | convolution fusion | flops 4432429056 | bytes 23920640 | tf_op jit(solution)/shard_map/nesf,efd->nesd/dot_general | solution.py:38
  300.0 114.4 %reduce-scatter.2.cloned.1.call-done = f32[64,1,24,512]{3,2,0,1:T(8,128)} async-done(((f32[64,1,24,2048]{3,2,0,1:T(8,128)}), f32[64,1,24,512]{3,2,0,1:T(8,128)}) %reduce-scatter.2.cloned.1.call-update) | async-done | bytes 3145744 | tf_op jit(solution)/shard_map/reduce_scatter | solution.py:196
  414.4 3.2 convert_bitcast_fusion
  417.7 10.9 %all-to-all-start.1 = ((bf16[64,1,24,512]{3,2,1,0:T(8,128)(2,1)}), bf16[64,1,24,512]{3,2,1,0:T(8,128)(2,1)}, u32[]{:S(2)}, u32[]{:S(2)}) async-start(bf16[64,1,24,512]{3,2,1,0:T(8,128)(2,1)} %convert_bitcast_fusion), calls=%async_computation.2 | async-start | bytes 3145728 | tf_op jit(solution)/shard_map/all_to_all | solution.py:42
  428.6 1.5 select_reduce_fusion
  430.2 37.4 %all-to-all-done.1 = bf16[64,1,24,512]{3,2,1,0:T(8,128)(2,1)} async-done(((bf16[64,1,24,512]{3,2,1,0:T(8,128)(2,1)}), bf16[64,1,24,512]{3,2,1,0:T(8,128)(2,1)}, u32[]{:S(2)}, u32[]{:S(2)}) %all-to-all-start.1) | async-done | bytes 1572896 | tf_op jit(solution)/shard_map/all_to_all | solution.py:42
  467.6 3.1 fusion.29
  (136 shorter events, 22.8 us)
Async XLA Ops:
  6.5 32.2 %copy-start = (bf16[2048,768]{1,0:T(8,128)(2,1)S(1)}, bf16[2048,768]{1,0:T(8,128)(2,1)}, u32[]{:S(2)}) copy-start(bf16[2048,768]{1,0:T(8,128)(2,1)} %param.20) | copy-start | bytes 9437188
  6.5 15.8 %copy-start.21 = (f32[512]{0:T(512)S(1)}, f32[512]{0:T(512)}, u32[]{:S(2)}) copy-start(f32[512]{0:T(512)} %param.22) | copy-start | bytes 6148
  6.5 18.3 %copy-start.23 = (s32[4]{0:T(128)S(1)}, s32[4]{0:T(128)}, u32[]{:S(2)}) copy-start(s32[4]{0:T(128)} %param.32) | copy-start | bytes 52
  6.5 118.6 %all-reduce.2.cloned.1.call-start = ((), (), s32[]{:S(2)}) async-start(), calls=%async_computation.3 | async-start | bytes 2097152 | tf_op jit(solution)/shard_map/psum | solution.py:180
  9.5 29.3 %copy-start.18 = (f32[2048]{0:T(1024)S(1)}, f32[2048]{0:T(1024)}, u32[]{:S(2)}) copy-start(f32[2048]{0:T(1024)} %param.19) | copy-start | bytes 24580
  42.9 2.8 copy-start.22
  42.9 2.8 copy-start.24
  44.0 6.1 %copy-start.6 = (bf16[128,4,576]{2,0,1:T(8,128)(2,1)}, bf16[128,4,576]{2,0,1:T(8,128)(2,1)S(1)}, u32[]{:S(2)}) copy-start(bf16[128,4,576]{2,0,1:T(8,128)(2,1)S(1)} %pad_maximum_fusion) | copy-start | bytes 1769476
  50.1 2.1 copy-start.5
  52.2 2.3 copy-start.10
  52.2 2.3 copy-start.11
  52.2 2.3 copy-start.12
  52.2 2.3 copy-start.13
  52.2 2.3 copy-start.14
  52.2 2.3 copy-start.15
  52.3 2.3 copy-start.16
  54.3 1.4 copy-start.27
  55.6 3.1 copy-start.7
  58.7 5.9 %slice-start = ((bf16[4,4,8,4,576]{4,2,0,3,1:T(8,128)(2,1)}), bf16[4,4,8,4,512]{4,2,0,3,1:T(8,128)(2,1)S(1)}, s32[]{:S(2)}) async-start(bf16[4,4,8,4,576]{4,2,0,3,1:T(8,128)(2,1)} %copy-done.7), calls=%async_computation.5 | async-start | bytes 1048576 | tf_op jit(solution)/shard_map/slice | solution.py:153
  64.6 1.7 copy-start.9
  67.3 1.8 copy-start.8
  69.0 1.8 copy-start.17
  70.5 54.6 %copy-start.4 = (bf16[128,2048]{1,0:T(8,128)(2,1)S(1)}, bf16[128,2048]{1,0:T(8,128)(2,1)}, u32[]{:S(2)}) copy-start(bf16[128,2048]{1,0:T(8,128)(2,1)} %param.18) | copy-start | bytes 1572868
  70.6 343.9 %reduce-scatter.2.cloned.1.call-start = ((), (), s32[]{:S(2)}) async-start(), calls=%async_computation.4 | async-start | bytes 15728640 | tf_op jit(solution)/shard_map/reduce_scatter | solution.py:196
  70.9 55.7 %copy-start.19 = (f32[2048]{0:T(1024)S(1)}, f32[2048]{0:T(1024)}, u32[]{:S(2)}) copy-start(f32[2048]{0:T(1024)} %param.26) | copy-start | bytes 24580
  126.6 1.9 copy-start.3
  128.5 154.2 %copy-start.25 = (bf16[1,2048,352]{1,2,0:T(8,128)(2,1)S(1)}, bf16[1,2048,352]{1,2,0:T(8,128)(2,1)}, u32[]{:S(2)}) copy-start(bf16[1,2048,352]{1,2,0:T(8,128)(2,1)} %param.27) | copy-start | bytes 4325380
  280.1 2.6 copy-start.2
  282.6 5.0 %copy-start.26 = (bf16[1,352,2048]{2,1,0:T(8,128)(2,1)S(1)}, bf16[1,352,2048]{2,1,0:T(8,128)(2,1)}, u32[]{:S(2)}) copy-start(bf16[1,352,2048]{2,1,0:T(8,128)(2,1)} %param.29) | copy-start | bytes 4325380
  417.7 11.0 %copy-start.20 = (f32[128,6]{0,1:T(8,128)S(1)}, f32[128,6]{0,1:T(8,128)}, u32[]{:S(2)}) copy-start(f32[128,6]{0,1:T(8,128)} %param.35) | copy-start | bytes 9220
  417.7 49.9 %all-to-all-start.1 = ((bf16[64,1,24,512]{3,2,1,0:T(8,128)(2,1)}), bf16[64,1,24,512]{3,2,1,0:T(8,128)(2,1)}, u32[]{:S(2)}, u32[]{:S(2)}) async-start(bf16[64,1,24,512]{3,2,1,0:T(8,128)(2,1)} %convert_bitcast_fusion), calls=%async_computation.2 | async-start | bytes 3145728 | tf_op jit(solution)/shard_map/all_to_all | solution.py:42
  428.6 42.1 %copy-start.1 = (bf16[2048,768]{1,0:T(8,128)(2,1)S(1)}, bf16[2048,768]{1,0:T(8,128)(2,1)}, u32[]{:S(2)}) copy-start(bf16[2048,768]{1,0:T(8,128)(2,1)} %param.20) | copy-start | bytes 9437188
Sparse Core Ops, SparseCore 0:
  70.7 54.3 all-reduce.1
  300.1 114.2 reduce-scatter.1
where the time goes:
time: 478 us
  waiting for transfers between devices  203 us (42%)
  blocking collectives  163 us (34%)
  matrix products  45.9 us (10%)
  other arithmetic  23 us (5%)
  local copies, waits for them, and re-layouts  18.1 us (4%)
  between operations  14 us (3%)
  starting transfers between devices  11.2 us (2%)
    all_to_all x1, blocking collectives, local(): lax.all_to_all(placed.reshape(req_count, EXP_DEV, capacity, moe_in.shape[...  152 us
    reduce_scatter x1, waiting for transfers between devices, local(): lax.psum_scatter(partial_out, 'tp', scatter_dimension=3, tiled=True)  114 us
    psum x1, waiting for transfers between devices, local(): attn_full = lax.psum(attn_part, 'tp')  50.8 us
    all_to_all x1, waiting for transfers between devices, send_home(): lax.all_to_all(shares, 'req', split_axis=0, concat_axis=0, tiled=True)  37.4 us
    dot_general x1, matrix products, expert_math(): jnp.einsum('nesf,efd->nesd', active, down_w, preferred_element_type=jnp.f...  12.3 us
    all_gather x1, blocking collectives, local(): kv_all = lax.all_gather(kv_part, 'tp', axis=1, tiled=True)  11.2 us
    all_to_all x1, starting transfers between devices, send_home(): lax.all_to_all(shares, 'req', split_axis=0, concat_axis=0, tiled=True)  10.9 us
  transfers between devices with their start and end apart: 3, of which 3 were waited for; matrix products, arithmetic and copies ran while one was open for 1% of the time, Pallas kernels for 0%

commit v1 on v0

--- a/solution.py
+++ b/solution.py
@@ -16,6 +16,12 @@
 PAGES = 8
 eps = 1e-06
 rope_base = 50000.0
+
+
+def gather_and_add(shard, name):
+    parts = lax.all_gather(shard, name, axis=0, tiled=False)
+    summed = parts.sum(axis=0)
+    return summed
 
 
 def rms_scale(values):
@@ -177,7 +183,7 @@
     weight_rows = jnp.sum(jnp.where(slot_hot, route_weights[:, :, None], 0.0), axis=1)
     tp_index = lax.axis_index("tp")
     col_start = tp_index * col_share
-    attn_full = lax.psum(attn_part, "tp")
+    attn_full = gather_and_add(attn_part, "tp")
     resid_full = hidden_f + attn_full
     moe_in = (resid_full * rms_scale(resid_full) * moe_gain).astype(jnp.bfloat16)
     placed = jnp.dot(gather_rows.T, moe_in, preferred_element_type=jnp.float32).astype(jnp.bfloat16)

time: 478 us -> 481 us (level)
    all_gather x0 -> x1, waiting for transfers between devices: none -> 52 us  [gather_and_add(): parts = lax.all_gather(shard, name, axis=0, tiled=False)]
    psum x1 -> x0, waiting for transfers between devices: 50.8 us -> none  [local(): attn_full = lax.psum(attn_part, 'tp')]
where the time goes in v1:
time: 481 us; the launch traced here: 480 us
  waiting for transfers between devices  203 us (42%)
  blocking collectives  161 us (33%)
  matrix products  45.9 us (10%)
  other arithmetic  26.7 us (6%)
  local copies, waits for them, and re-layouts  18.1 us (4%)
  between operations  13.9 us (3%)
  starting transfers between devices  11.2 us (2%)
    all_to_all x1, blocking collectives, local(): lax.all_to_all(placed.reshape(req_count, EXP_DEV, capacity, moe_in.shape[...  150 us
    reduce_scatter x1, waiting for transfers between devices, local(): lax.psum_scatter(partial_out, 'tp', scatter_dimension=3, tiled=True)  114 us
    all_gather x1, waiting for transfers between devices, gather_and_add(): parts = lax.all_gather(shard, name, axis=0, tiled=False)  52 us
    all_to_all x1, waiting for transfers between devices, send_home(): lax.all_to_all(shares, 'req', split_axis=0, concat_axis=0, tiled=True)  37.4 us
    dot_general x1, matrix products, expert_math(): jnp.einsum('nesf,efd->nesd', active, down_w, preferred_element_type=jnp.f...  12.3 us
    all_gather x1, blocking collectives, local(): kv_all = lax.all_gather(kv_part, 'tp', axis=1, tiled=True)  11.2 us
    all_to_all x1, starting transfers between devices, send_home(): lax.all_to_all(shares, 'req', split_axis=0, concat_axis=0, tiled=True)  10.9 us
  transfers between devices with their start and end apart: 3, of which 3 were waited for; matrix products, arithmetic and copies ran while one was open for 1% of the time, Pallas kernels for 0%

profile of v1, /device:TPU:1, one launch (start us, length us, event | category | flops | bytes accessed | tf_op | source)
XLA Modules:
  0.0 480.4 jit_solution(8657390105484211253)
XLA Ops:
  8.2 1.2 fusion.40
  9.5 1.6 fusion.63
  11.1 11.2 %all_gather.9 = f32[128,576]{0,1:T(8,128)S(1)} all-gather(f32[128,144]{0,1:T(8,128)S(1)} %fusion.63), channel_id=1, replica_groups=mesh['req'=64,'tp'=4] {'tp'}, dimensions={1}, use_global_device_ids=true | all-gather | bytes 368640 | tf_op jit(solution)/shard_map/all_gather | solution.py:98
  23.2 1.6 copy.150
  38.8 2.4 fusion.65
  41.5 1.4 fusion.22
  44.5 1.2 reshape.300
  46.0 4.1 gather_fusion
  50.1 2.1 bitcast_select_fusion
  52.3 2.0 fusion.86
  55.6 3.1 fusion.87
  59.0 1.2 fusion.58
  60.2 2.6 reshape.302
  62.8 1.5 exponential_reduce_fusion
  64.6 1.7 fusion.51
  67.3 1.4 copy.179
  69.1 1.4 fusion.88
  71.2 1.8 reduce-window.6
  74.3 52.0 %all-gather.3.cloned.1.call-done = f32[512,2048]{1,0:T(8,128)} async-done(((f32[128,2048]{1,0:T(8,128)}), f32[512,2048]{1,0:T(8,128)}) %all-gather.3.cloned.1.call-update) | async-done | bytes 4194320 | tf_op jit(solution)/shard_map/all_gather | solution.py:22
  126.3 3.6 reduce_sum.90
  129.9 1.5 multiply_reduce_fusion
  131.4 1.9 convolution_convert_fusion
  133.3 150.2 %all_to_all.10 = bf16[64,1,24,2048]{3,2,1,0:T(8,128)(2,1)S(1)} all-to-all(bf16[64,1,24,2048]{3,2,1,0:T(8,128)(2,1)S(1)} %bitcast.217), channel_id=1, replica_groups=mesh['req'=64,'tp'=4] {'req'}, dimensions={0} | all-to-all | bytes 12582912 | tf_op jit(solution)/shard_map/all_to_all | solution.py:191
  283.5 2.6 copy-done.2
  286.1 5.0 %fusion.2 = f32[64,24,352]{2,1,0:T(8,128)} fusion(bf16[64,1,24,2048]{3,2,1,0:T(8,128)(2,1)S(1)} %all_to_all.10, bf16[1,2048,352]{1,2,0:T(8,128)(2,1)S(1)} %copy-done.25), kind=kOutput, calls=%fused_computation.4 | convolution fusion | flops 2214592512 | bytes 9895936 | tf_op jit(solution)/shard_map/nesd,edf->nesf/dot_general | solution.py:41
  291.1 12.3 %convolution_bitcast_fusion = f32[64,1,24,2048]{3,2,0,1:T(8,128)} fusion(bf16[1,352,2048]{2,1,0:T(8,128)(2,1)S(1)} %copy-done.26, bf16[1,2048,352]{1,2,0:T(8,128)(2,1)} %param.28, bf16[64,1,24,2048]{3,2,1,0:T(8,128)(2,1)} %copy-done.2, f32[64,24,352]{2,1,0:T(8,128)} %fusion.2), kind=kOutput, calls=%fused_computation.6 | convolution fusion | flops 4432429056 | bytes 23920640 | tf_op jit(solution)/shard_map/nesf,efd->nesd/dot_general | solution.py:44
  303.4 113.9 %reduce-scatter.2.cloned.1.call-done = f32[64,1,24,512]{3,2,0,1:T(8,128)} async-done(((f32[64,1,24,2048]{3,2,0,1:T(8,128)}), f32[64,1,24,512]{3,2,0,1:T(8,128)}) %reduce-scatter.2.cloned.1.call-update) | async-done | bytes 3145744 | tf_op jit(solution)/shard_map/reduce_scatter | solution.py:202
  417.3 3.2 convert_bitcast_fusion
  420.6 10.9 %all-to-all-start.1 = ((bf16[64,1,24,512]{3,2,1,0:T(8,128)(2,1)}), bf16[64,1,24,512]{3,2,1,0:T(8,128)(2,1)}, u32[]{:S(2)}, u32[]{:S(2)}) async-start(bf16[64,1,24,512]{3,2,1,0:T(8,128)(2,1)} %convert_bitcast_fusion), calls=%async_computation.2 | async-start | bytes 3145728 | tf_op jit(solution)/shard_map/all_to_all | solution.py:48
  431.6 1.5 select_reduce_fusion
  433.1 37.4 %all-to-all-done.1 = bf16[64,1,24,512]{3,2,1,0:T(8,128)(2,1)} async-done(((bf16[64,1,24,512]{3,2,1,0:T(8,128)(2,1)}), bf16[64,1,24,512]{3,2,1,0:T(8,128)(2,1)}, u32[]{:S(2)}, u32[]{:S(2)}) %all-to-all-start.1) | async-done | bytes 1572896 | tf_op jit(solution)/shard_map/all_to_all | solution.py:48
  470.5 3.1 fusion.29
  (137 shorter events, 23.8 us)
Async XLA Ops:
  6.5 32.2 %copy-start = (bf16[2048,768]{1,0:T(8,128)(2,1)S(1)}, bf16[2048,768]{1,0:T(8,128)(2,1)}, u32[]{:S(2)}) copy-start(bf16[2048,768]{1,0:T(8,128)(2,1)} %param.20) | copy-start | bytes 9437188
  6.5 15.8 %copy-start.21 = (f32[512]{0:T(512)S(1)}, f32[512]{0:T(512)}, u32[]{:S(2)}) copy-start(f32[512]{0:T(512)} %param.22) | copy-start | bytes 6148
  6.5 18.3 %copy-start.23 = (s32[4]{0:T(128)S(1)}, s32[4]{0:T(128)}, u32[]{:S(2)}) copy-start(s32[4]{0:T(128)} %param.32) | copy-start | bytes 52
  6.5 119.7 %all-gather.3.cloned.1.call-start = ((), (), s32[]{:S(2)}) async-start(), calls=%async_computation.4 | async-start | bytes 5242880 | tf_op jit(solution)/shard_map/all_gather | solution.py:22
  9.5 29.3 %copy-start.18 = (f32[2048]{0:T(1024)S(1)}, f32[2048]{0:T(1024)}, u32[]{:S(2)}) copy-start(f32[2048]{0:T(1024)} %param.19) | copy-start | bytes 24580
  42.9 2.8 copy-start.22
  42.9 2.8 copy-start.24
  44.0 6.1 %copy-start.6 = (bf16[128,4,576]{2,0,1:T(8,128)(2,1)}, bf16[128,4,576]{2,0,1:T(8,128)(2,1)S(1)}, u32[]{:S(2)}) copy-start(bf16[128,4,576]{2,0,1:T(8,128)(2,1)S(1)} %pad_maximum_fusion) | copy-start | bytes 1769476
  50.1 2.1 copy-start.5
  52.2 2.3 copy-start.10
  52.2 2.3 copy-start.11
  52.2 2.3 copy-start.12
  52.2 2.3 copy-start.13
  52.2 2.3 copy-start.14
  52.2 2.3 copy-start.15
  52.3 2.3 copy-start.16
  54.3 1.4 copy-start.27
  55.6 3.1 copy-start.7
  58.7 5.9 %slice-start = ((bf16[4,4,8,4,576]{4,2,0,3,1:T(8,128)(2,1)}), bf16[4,4,8,4,512]{4,2,0,3,1:T(8,128)(2,1)S(1)}, s32[]{:S(2)}) async-start(bf16[4,4,8,4,576]{4,2,0,3,1:T(8,128)(2,1)} %copy-done.7), calls=%async_computation.5 | async-start | bytes 1048576 | tf_op jit(solution)/shard_map/slice | solution.py:159
  64.6 1.7 copy-start.9
  67.3 1.8 copy-start.8
  69.0 1.7 copy-start.17
  70.5 346.8 %reduce-scatter.2.cloned.1.call-start = ((), (), s32[]{:S(2)}) async-start(), calls=%async_computation.3 | async-start | bytes 15728640 | tf_op jit(solution)/shard_map/reduce_scatter | solution.py:202
  126.3 3.6 copy-start.4
  129.9 1.5 copy-start.19
  131.4 1.9 copy-start.3
  133.3 152.8 %copy-start.25 = (bf16[1,2048,352]{1,2,0:T(8,128)(2,1)S(1)}, bf16[1,2048,352]{1,2,0:T(8,128)(2,1)}, u32[]{:S(2)}) copy-start(bf16[1,2048,352]{1,2,0:T(8,128)(2,1)} %param.27) | copy-start | bytes 4325380
  283.5 2.6 copy-start.2
  286.1 5.0 %copy-start.26 = (bf16[1,352,2048]{2,1,0:T(8,128)(2,1)S(1)}, bf16[1,352,2048]{2,1,0:T(8,128)(2,1)}, u32[]{:S(2)}) copy-start(bf16[1,352,2048]{2,1,0:T(8,128)(2,1)} %param.29) | copy-start | bytes 4325380
  420.6 11.0 %copy-start.20 = (f32[128,6]{0,1:T(8,128)S(1)}, f32[128,6]{0,1:T(8,128)}, u32[]{:S(2)}) copy-start(f32[128,6]{0,1:T(8,128)} %param.35) | copy-start | bytes 9220
  420.6 49.9 %all-to-all-start.1 = ((bf16[64,1,24,512]{3,2,1,0:T(8,128)(2,1)}), bf16[64,1,24,512]{3,2,1,0:T(8,128)(2,1)}, u32[]{:S(2)}, u32[]{:S(2)}) async-start(bf16[64,1,24,512]{3,2,1,0:T(8,128)(2,1)} %convert_bitcast_fusion), calls=%async_computation.2 | async-start | bytes 3145728 | tf_op jit(solution)/shard_map/all_to_all | solution.py:48
  431.5 42.1 %copy-start.1 = (bf16[2048,768]{1,0:T(8,128)(2,1)S(1)}, bf16[2048,768]{1,0:T(8,128)(2,1)}, u32[]{:S(2)}) copy-start(bf16[2048,768]{1,0:T(8,128)(2,1)} %param.20) | copy-start | bytes 9437188
Sparse Core Ops, SparseCore 0:
  70.6 55.6 all-gather.2
  303.5 113.7 reduce-scatter.1
